TPU v7x, 128 devices: a whole 4x4x4 slice. The times are simulated.
128 devices in a mesh: row: 32 (over y, z_lo, x), col: 4 (over z_hi, core).
Axes of the slice: x: 4, y: 4, z: 4 (z_hi: 2, z_lo: 2; z = z_hi * 2 + z_lo), core: 2. Of those that a mesh axis runs over, the one named last changes fastest.
Arguments:
- ratings: bfloat16 [4, 262144, 512], P(None, ('row', 'col'))
- tile_mask: int32 [4, 2048, 4], P(None, ('row', 'col')), may hold values from 0 to 1, as said below
- tile_counts: int32 [128], replicated, may hold values from 1 to 16, as said below
- users: float32 [131072, 128], P(('row', 'col')), may hold values from -2 to 2
- user_accum: float32 [131072, 128], P(('row', 'col')), may hold values from 0.05 to 0.5
- items: float32 [65536, 128], P(('row', 'col')), may hold values from -2 to 2
- item_accum: float32 [65536, 128], P(('row', 'col')), may hold values from 0.05 to 0.5
Outputs:
- users_out: float32 [131072, 128], P(('row', 'col'))
- user_accum_out: float32 [131072, 128], P(('row', 'col'))
- items_out: float32 [65536, 128], P(('row', 'col'))
- item_accum_out: float32 [65536, 128], P(('row', 'col'))
- losses: float32 [4], replicated
Inputs may be any that keep to these rules, and one draw needn't show every extreme that they name: Each group of 4 positions has tile_counts summing to 32, and exactly one position of each group, not always the same, owns 2 * 8 tiles. `tile_mask`: in each stratum, the first slot's first item tile of every position is 1.
All inputs are finite; a program needn't handle non-finite values.
Results may differ from a plain program's by a relative error of at most 0.0025.
Values sent between devices are 32-bit elements; how exact they have to be, the bound alone decides.
No kernel may reach another device: no remote copies, remote signals or barrier semaphores. Data moves between devices by JAX's collectives and lax.ppermute only.
A program may use at most 64 MiB of HBM per device.

v0:
```python
import jax
import jax.numpy as jnp
from jax import lax
from jax.sharding import PartitionSpec as P

TILE = 128
UT = 8
STEPS = 3
ridge_weight = 0.02
step_rate = 0.05


def passed_along(value, axis, steps):
    count = lax.axis_size(axis)
    pairs = [(source, (source + steps) % count) for source in range(count)]
    return lax.ppermute(value, axis, pairs)


def update(user_fac, user_acc, item_fac, item_acc, rating_block, live_tiles):
    tile_size = user_fac.shape[0] // live_tiles.shape[0]
    user_half = user_fac.astype(jnp.bfloat16)
    item_half = item_fac.astype(jnp.bfloat16)
    predicted = lax.dot_general(
        user_half, item_half, (((1,), (1,)), ((), ())), preferred_element_type=jnp.float32
    )
    residue = predicted - rating_block.astype(jnp.float32)
    masked = (
        residue.reshape(live_tiles.shape[0], tile_size, live_tiles.shape[1], tile_size)
        * live_tiles[:, None, :, None]
    ).reshape(residue.shape)
    sq_error = jnp.sum(masked * residue)
    err_half = masked.astype(jnp.bfloat16)
    grad_user = (
        jnp.dot(err_half, item_half, preferred_element_type=jnp.float32)
        * float(item_fac.shape[0]) ** (-0.5)
        + ridge_weight * user_fac
    )
    grad_item = (
        lax.dot_general(
            err_half, user_half, (((0,), (0,)), ((), ())), preferred_element_type=jnp.float32
        )
        * float(UT * TILE) ** (-0.5)
        + ridge_weight * item_fac
    )
    user_acc = user_acc + grad_user * grad_user
    item_acc = item_acc + grad_item * grad_item
    user_fac = user_fac - step_rate * grad_user * lax.rsqrt(user_acc)
    item_fac = item_fac - step_rate * grad_item * lax.rsqrt(item_acc)
    return (user_fac, user_acc, item_fac, item_acc, sq_error)


def on_device(ratings, tile_mask, tile_counts, users, user_accum, items, item_accum):
    strata_count = ratings.shape[0]
    slot_count = tile_mask.shape[1]
    tile_size = ratings.shape[1] // slot_count
    group_size = lax.axis_size("col")
    member = lax.axis_index("col")
    arrived_rows = users.shape[0]
    group_counts = lax.dynamic_slice_in_dim(
        tile_counts, lax.axis_index("row") * group_size, group_size
    )
    ranks = jnp.arange(group_size, dtype=jnp.int32)
    start_tile = jnp.sum(jnp.where(ranks < member, group_counts, 0))
    own_count = jnp.sum(jnp.where(ranks == member, group_counts, 0))
    valid = (jnp.arange(slot_count, dtype=jnp.int32) < own_count).astype(jnp.float32)
    whole_fac, whole_acc = (
        lax.all_gather(users, "col", axis=0, tiled=True),
        lax.all_gather(user_accum, "col", axis=0, tiled=True),
    )
    pad_rows = slot_count * tile_size
    ext_fac = jnp.concatenate([whole_fac, whole_fac[:pad_rows]], axis=0)
    ext_acc = jnp.concatenate([whole_acc, whole_acc[:pad_rows]], axis=0)
    user_fac = lax.dynamic_slice_in_dim(ext_fac, start_tile * tile_size, pad_rows, 0)
    user_acc = lax.dynamic_slice_in_dim(ext_acc, start_tile * tile_size, pad_rows, 0)
    held_pair = jnp.stack([items, item_accum])
    loss_list = []
    for stratum in range(strata_count):
        live_tiles = tile_mask[stratum].astype(jnp.float32) * valid[:, None]
        item_fac = held_pair[0]
        item_acc = held_pair[1]
        for inner in range(STEPS):
            user_fac, user_acc, item_fac, item_acc, sq_error = update(
                user_fac, user_acc, item_fac, item_acc, ratings[stratum], live_tiles
            )
            if inner == 0:
                observed = jnp.sum(live_tiles) * float(tile_size * tile_size)
                total_error, total_count = lax.psum((sq_error, observed), ("row", "col"))
                loss_list.append(total_error / total_count)
        held_pair = jnp.stack([item_fac, item_acc])
        if stratum + 1 < strata_count:
            held_pair = passed_along(held_pair, ("row", "col"), 1)
    losses = jnp.stack(loss_list)
    row_valid = jnp.repeat(valid, tile_size)[:, None] > 0.5
    kept_fac = jnp.where(row_valid, user_fac, 0.0)
    kept_acc = jnp.where(row_valid, user_acc, 0.0)
    frame_rows = group_size * arrived_rows + pad_rows
    frame_fac = lax.dynamic_update_slice_in_dim(
        jnp.zeros((frame_rows, kept_fac.shape[1]), jnp.float32), kept_fac, start_tile * tile_size, 0
    )
    frame_acc = lax.dynamic_update_slice_in_dim(
        jnp.zeros((frame_rows, kept_acc.shape[1]), jnp.float32), kept_acc, start_tile * tile_size, 0
    )
    users_new, accum_new = (
        lax.psum_scatter(
            frame_fac[: group_size * arrived_rows], "col", scatter_dimension=0, tiled=True
        ),
        lax.psum_scatter(
            frame_acc[: group_size * arrived_rows], "col", scatter_dimension=0, tiled=True
        ),
    )
    return (users_new, accum_new, held_pair[0], held_pair[1], losses)


def solution(mesh):
    return jax.shard_map(
        on_device,
        mesh=mesh,
        in_specs=(
            P(None, ("row", "col"), None),
            P(None, ("row", "col"), None),
            P(),
            P(("row", "col"), None),
            P(("row", "col"), None),
            P(("row", "col"), None),
            P(("row", "col"), None),
        ),
        out_specs=(
            P(("row", "col"), None),
            P(("row", "col"), None),
            P(("row", "col"), None),
            P(("row", "col"), None),
            P(),
        ),
        check_vma=False,
    )
```

profile of v0, /device:TPU:0, one launch (start us, length us, event | category | flops | bytes accessed | tf_op | source)
XLA Modules:
  0.0 266.9 jit_solution(3098577988542652203)
XLA Ops:
  12.9 26.0 %all-gather.3.cloned.1.call-done = f32[4096,128]{1,0:T(8,128)} async-done(((f32[1024,128]{1,0:T(8,128)}), f32[4096,128]{1,0:T(8,128)}) %all-gather.3.cloned.1.call-update) | async-done | bytes 2097168 | tf_op jit(solution)/shard_map/all_gather | solution.py:67
  40.1 1.6 fusion.37
  42.7 4.7 %multiply_reduce_fusion.3 = (f32[]{:T(128)}, bf16[2048,512]{1,0:T(8,128)(2,1)S(1)}) fusion(f32[256,8,4,128]{3,2,1,0:T(4,128)S(1)} %bitcast.197, bf16[4,2048,512]{2,1,0:T(8,128)(2,1)} %param.7, f32[512,128]{1,0:T(8,128)S(1)} %copy-done.8, f32[2048,128]{1,0:T(8,128)S(1)} %fusion.37), kind=kOutput, calls=%fused_computation.35 | convolution fusion | flops 275054592 | bytes 9699332 | tf_op jit(solution)/shard_map/dot_general | solution.py:23
  48.9 17.7 %all-gather.5.cloned.1.call-done = f32[4096,128]{1,0:T(8,128)} async-done(((f32[1024,128]{1,0:T(8,128)}), f32[4096,128]{1,0:T(8,128)}) %all-gather.5.cloned.1.call-update) | async-done | bytes 2097168 | tf_op jit(solution)/shard_map/all_gather | solution.py:68
  67.8 2.2 multiply_subtract_fusion.10
  70.3 2.4 fusion.1
  73.5 1.7 multiply_subtract_fusion.9
  75.2 2.3 fusion.3
  79.4 2.3 multiply_subtract_fusion.8
  81.8 11.7 %collective-permute-done = f32[2,512,128]{2,1,0:T(8,128)} collective-permute-done((f32[2,512,128]{2,1,0:T(8,128)}, f32[2,512,128]{2,1,0:T(8,128)}, u32[]{:S(2)}, u32[]{:S(2)}) %collective-permute-start) | collective-permute-done | bytes 524320 | tf_op jit(solution)/shard_map/ppermute | solution.py:16
  94.1 3.7 %multiply_reduce_fusion.2 = (f32[]{:T(128)}, bf16[2048,512]{1,0:T(8,128)(2,1)S(1)}) fusion(f32[256,8,4,128]{3,2,1,0:T(4,128)S(1)} %bitcast.200, bf16[4,2048,512]{2,1,0:T(8,128)(2,1)} %param.7, f32[2,512,128]{2,1,0:T(8,128)} %collective-permute-done, f32[2048,128]{1,0:T(8,128)S(1)} %get-tuple-element.33), kind=kOutput, calls=%fused_computation.34 | convolution fusion | flops 274989056 | bytes 9568260 | tf_op jit(solution)/shard_map/dot_general | solution.py:23
  97.8 1.9 multiply_subtract_fusion.17
  99.8 1.7 multiply_subtract_fusion.7
  102.2 1.7 multiply_subtract_fusion.6
  103.9 1.7 multiply_subtract_fusion.16
  109.7 1.9 multiply_subtract_fusion.5
  111.7 11.7 %collective-permute-done.1 = f32[2,512,128]{2,1,0:T(8,128)} collective-permute-done((f32[2,512,128]{2,1,0:T(8,128)}, f32[2,512,128]{2,1,0:T(8,128)}, u32[]{:S(2)}, u32[]{:S(2)}) %collective-permute-start.1) | collective-permute-done | bytes 524320 | tf_op jit(solution)/shard_map/ppermute | solution.py:16
  124.0 3.7 %multiply_reduce_fusion.1 = (f32[]{:T(128)}, bf16[2048,512]{1,0:T(8,128)(2,1)S(1)}) fusion(f32[256,8,4,128]{3,2,1,0:T(4,128)S(1)} %bitcast.203, bf16[4,2048,512]{2,1,0:T(8,128)(2,1)} %param.7, f32[2,512,128]{2,1,0:T(8,128)} %collective-permute-done.1, f32[2048,128]{1,0:T(8,128)S(1)} %get-tuple-element.69), kind=kOutput, calls=%fused_computation.33 | convolution fusion | flops 274989056 | bytes 9568260 | tf_op jit(solution)/shard_map/dot_general | solution.py:23
  127.6 1.9 multiply_subtract_fusion.15
  129.6 1.7 multiply_subtract_fusion.4
  132.2 1.7 multiply_subtract_fusion.3
  134.0 1.7 multiply_subtract_fusion.14
  139.2 2.3 multiply_subtract_fusion.2
  141.5 11.9 %collective-permute-done.2 = f32[2,512,128]{2,1,0:T(8,128)} collective-permute-done((f32[2,512,128]{2,1,0:T(8,128)}, f32[2,512,128]{2,1,0:T(8,128)}, u32[]{:S(2)}, u32[]{:S(2)}) %collective-permute-start.2) | collective-permute-done | bytes 524320 | tf_op jit(solution)/shard_map/ppermute | solution.py:16
  154.0 3.7 %multiply_reduce_fusion = (f32[]{:T(128)}, bf16[2048,512]{1,0:T(8,128)(2,1)S(1)}) fusion(f32[256,8,4,128]{3,2,1,0:T(4,128)S(1)} %bitcast.206, bf16[4,2048,512]{2,1,0:T(8,128)(2,1)} %param.7, f32[2,512,128]{2,1,0:T(8,128)} %collective-permute-done.2, f32[2048,128]{1,0:T(8,128)S(1)} %get-tuple-element.27), kind=kOutput, calls=%fused_computation.32 | convolution fusion | flops 274989056 | bytes 9568260 | tf_op jit(solution)/shard_map/dot_general | solution.py:23
  157.7 1.9 multiply_subtract_fusion.13
  159.7 1.8 multiply_subtract_fusion.1
  163.0 2.4 multiply_subtract_fusion.12
  167.0 1.6 copy-done.5
  170.8 3.1 %slice.88 = f32[4096,128]{1,0:T(8,128)} slice(f32[6144,128]{1,0:T(8,128)} %copy-done.5), slice={[0:4096], [0:128]} | slice | bytes 4194304 | tf_op jit(solution)/shard_map/slice | solution.py:105
  176.4 75.4 %all-reduce = (f32[]{:T(128)}, f32[]{:T(128)}, f32[]{:T(128)}, f32[]{:T(128)}, f32[]{:T(128)}, /*index=5*/f32[]{:T(128)}, f32[]{:T(128)}, f32[]{:T(128)}) all-reduce(f32[]{:T(128)} %get-tuple-element.45, f32[]{:T(128)S(6)} %mul.689, f32[]{:T(128)} %get-tuple-element.43, ...), channel_id=1, replica_groups=mesh['row'=32,'col'=4] {'row','col'}, use_global_device_ids=true, to_apply=%region_17.18 | all-reduce | flops 8 | bytes 64 | tf_op jit(solution)/shard_map/psum | solution.py:87
  257.7 2.6 multiply_subtract_fusion.11
  (93 shorter events, 29.7 us)
Async XLA Ops:
  7.2 31.8 %all-gather.3.cloned.1.call-start = ((), (), s32[]{:S(2)}) async-start(), calls=%async_computation.2 | async-start | bytes 2621440 | tf_op jit(solution)/shard_map/all_gather | solution.py:67
  7.9 58.7 %all-gather.5.cloned.1.call-start = ((), (), s32[]{:S(2)}) async-start(), calls=%async_computation.3 | async-start | bytes 2621440 | tf_op jit(solution)/shard_map/all_gather | solution.py:68
  8.6 251.7 %reduce-scatter.5.cloned.1.call-start = ((), (), s32[]{:S(2)}) async-start(), calls=%async_computation.5 | async-start | bytes 2621440 | tf_op jit(solution)/shard_map/reduce_scatter | solution.py:107
  38.9 1.2 slice-start.7
  41.8 1.0 copy-start.8
  42.4 5.0 %copy-start = (f32[16,128,4,128]{3,2,1,0:T(4,128)}, f32[16,128,4,128]{3,2,1,0:T(4,128)S(1)}, u32[]{:S(2)}) copy-start(f32[16,128,4,128]{3,2,1,0:T(4,128)S(1)} %mul.539) | copy-start | bytes 12582916
  42.7 4.7 %copy-start.10 = (f32[512,128]{1,0:T(8,128)S(1)}, f32[512,128]{1,0:T(8,128)}, u32[]{:S(2)}) copy-start(f32[512,128]{1,0:T(8,128)} %param.13) | copy-start | bytes 786436
  66.6 1.2 slice-start.6
  66.6 1.3 copy-start.9
  67.8 2.5 copy-start.1
  70.0 3.5 %copy-start.2 = (f32[2048,128]{1,0:T(8,128)}, f32[2048,128]{1,0:T(8,128)S(1)}, u32[]{:S(2)}) copy-start(f32[2048,128]{1,0:T(8,128)S(1)} %get-tuple-element.38) | copy-start | bytes 3145732
  70.3 2.4 copy-start.11
  70.3 2.4 copy-start.12
  73.5 4.0 %copy-start.6 = (f32[512,128]{1,0:T(8,128)}, f32[512,128]{1,0:T(8,128)S(1)}, u32[]{:S(2)}) copy-start(f32[512,128]{1,0:T(8,128)S(1)} %get-tuple-element.35) | copy-start | bytes 786436
  79.1 14.4 %collective-permute-start = (f32[2,512,128]{2,1,0:T(8,128)}, f32[2,512,128]{2,1,0:T(8,128)}, u32[]{:S(2)}, u32[]{:S(2)}) collective-permute-start(f32[2,512,128]{2,1,0:T(8,128)} %pad_maximum_fusion), channel_id=1, source_target_pairs={{0,1},{1,2},{2,3},{3,4},{4,5},{5,6},{6,7},{7,8},{8,9},{9,10},{10,1... | collective-permute-start | bytes 1572872 | tf_op jit(solution)/shard_map/ppermute | solution.py:16
  94.1 7.4 %slice-start = ((s8[8388608]{0:T(1024)(128)(4,1)}), s8[4194304]{0:T(1024)(128)(4,1)S(1)}, s32[]{:S(2)}) async-start(s8[8388608]{0:T(1024)(128)(4,1)} %bitcast.191), calls=%async_computation.6 | async-start | bytes 8388608
  97.8 3.6 %slice-start.1 = ((s8[8388608]{0:T(1024)(128)(4,1)}), s8[4194304]{0:T(1024)(128)(4,1)S(1)}, s32[]{:S(2)}) async-start(s8[8388608]{0:T(1024)(128)(4,1)} %bitcast.191), calls=%async_computation.7 | async-start | bytes 8388608
  109.0 14.4 %collective-permute-start.1 = (f32[2,512,128]{2,1,0:T(8,128)}, f32[2,512,128]{2,1,0:T(8,128)}, u32[]{:S(2)}, u32[]{:S(2)}) collective-permute-start(f32[2,512,128]{2,1,0:T(8,128)} %pad_maximum_fusion.1), channel_id=1, source_target_pairs={{0,1},{1,2},{2,3},{3,4},{4,5},{5,6},{6,7},{7,8},{8,9},{9,10},{10,1... | collective-permute-start | bytes 1572872 | tf_op jit(solution)/shard_map/ppermute | solution.py:16
  123.9 7.4 %slice-start.2 = ((s8[8388608]{0:T(1024)(128)(4,1)}), s8[4194304]{0:T(1024)(128)(4,1)S(1)}, s32[]{:S(2)}) async-start(s8[8388608]{0:T(1024)(128)(4,1)} %bitcast.193), calls=%async_computation.8 | async-start | bytes 8388608
  127.6 1.9 copy-start.3
  127.6 3.7 %slice-start.3 = ((s8[8388608]{0:T(1024)(128)(4,1)}), s8[4194304]{0:T(1024)(128)(4,1)S(1)}, s32[]{:S(2)}) async-start(s8[8388608]{0:T(1024)(128)(4,1)} %bitcast.193), calls=%async_computation.9 | async-start | bytes 8388608
  131.3 1.0 copy-start.4
  139.0 14.4 %collective-permute-start.2 = (f32[2,512,128]{2,1,0:T(8,128)}, f32[2,512,128]{2,1,0:T(8,128)}, u32[]{:S(2)}, u32[]{:S(2)}) collective-permute-start(f32[2,512,128]{2,1,0:T(8,128)} %pad_maximum_fusion.2), channel_id=1, source_target_pairs={{0,1},{1,2},{2,3},{3,4},{4,5},{5,6},{6,7},{7,8},{8,9},{9,10},{10,1... | collective-permute-start | bytes 1572872 | tf_op jit(solution)/shard_map/ppermute | solution.py:16
  154.0 7.5 %slice-start.4 = ((s8[8388608]{0:T(1024)(128)(4,1)}), s8[4194304]{0:T(1024)(128)(4,1)S(1)}, s32[]{:S(2)}) async-start(s8[8388608]{0:T(1024)(128)(4,1)} %bitcast.195), calls=%async_computation.10 | async-start | bytes 8388608
  157.7 3.7 %slice-start.5 = ((s8[8388608]{0:T(1024)(128)(4,1)}), s8[4194304]{0:T(1024)(128)(4,1)S(1)}, s32[]{:S(2)}) async-start(s8[8388608]{0:T(1024)(128)(4,1)} %bitcast.195), calls=%async_computation.11 | async-start | bytes 8388608
  159.7 3.3 %copy-start.7 = (f32[512,128]{1,0:T(8,128)}, f32[512,128]{1,0:T(8,128)S(1)}, u32[]{:S(2)}) copy-start(f32[512,128]{1,0:T(8,128)S(1)} %get-tuple-element.80) | copy-start | bytes 786436
  167.0 1.6 copy-start.5
  170.7 89.7 %reduce-scatter.3.cloned.1.call-start = ((), (), s32[]{:S(2)}) async-start(), calls=%async_computation.4 | async-start | bytes 2621440 | tf_op jit(solution)/shard_map/reduce_scatter | solution.py:104
Sparse Core Ops, SparseCore 0:
  9.6 29.2 all-gather.2
  40.6 25.9 all-gather.4
  170.8 31.6 reduce-scatter.4
  205.6 37.6 reduce-scatter.2
where the time goes:
time: 268 us; the launch traced here: 267 us
  waiting for transfers between devices  80.4 us (30%)
  blocking collectives  75.4 us (28%)
  matrix products  64 us (24%)
  between operations  22.7 us (8%)
  local copies, waits for them, and re-layouts  12.8 us (5%)
  other arithmetic  11.2 us (4%)
    psum x1, blocking collectives, on_device(): total_error, total_count = lax.psum((sq_error, observed), ('row', 'col'))  75.4 us
    ppermute x3, waiting for transfers between devices, passed_along(): return lax.ppermute(value, axis, pairs)  35.3 us
    all_gather x1, waiting for transfers between devices, on_device(): lax.all_gather(users, 'col', axis=0, tiled=True)  26 us
    dot_general x12, matrix products, update(): lax.dot_general(user_half, item_half, (((1,), (1,)), ((), ())), preferred...  24.8 us
    dot_general x12, matrix products, update(): jnp.dot(err_half, item_half, preferred_element_type=jnp.float32)  20.4 us
    dot_general x12, matrix products, update(): lax.dot_general(err_half, user_half, (((0,), (0,)), ((), ())), preferred_...  18.7 us
    all_gather x1, waiting for transfers between devices, on_device(): lax.all_gather(user_accum, 'col', axis=0, tiled=True)  17.7 us
  transfers between devices with their start and end apart: 7, of which 5 were waited for; matrix products, arithmetic and copies ran while one was open for 10% of the time, Pallas kernels for 0%

commit v1 on v0

--- a/solution.py
+++ b/solution.py
@@ -65,7 +65,9 @@
     valid = (jnp.arange(slot_count, dtype=jnp.int32) < own_count).astype(jnp.float32)
     whole_fac, whole_acc = (
         lax.all_gather(users, "col", axis=0, tiled=True),
-        lax.all_gather(user_accum, "col", axis=0, tiled=True),
+        jnp.concatenate(
+            lax.all_to_all(jnp.stack([user_accum] * lax.axis_size("col")), "col", 0, 0), axis=0
+        ),
     )
     pad_rows = slot_count * tile_size
     ext_fac = jnp.concatenate([whole_fac, whole_fac[:pad_rows]], axis=0)

time: 268 us -> 258 us (0.963)
  waiting for transfers between devices: 80.4 us -> 71.9 us
  matrix products: 64 us -> 57.5 us
  starting transfers between devices: 0.39 us -> 5.48 us
    all_to_all x0 -> x1, waiting for transfers between devices: none -> 35.6 us  [on_device(): lax.all_to_all(jnp.stack([user_accum] * lax.axis_size('col')), 'col', 0, 0)]
    all_gather x1, waiting for transfers between devices: 26 us -> 0.02 us  [on_device(): lax.all_gather(users, 'col', axis=0, tiled=True)]
    all_gather x1 -> x0, waiting for transfers between devices: 17.7 us -> none  [on_device(): lax.all_gather(user_accum, 'col', axis=0, tiled=True)]
    all_to_all x0 -> x1, starting transfers between devices: none -> 5.39 us  [on_device(): lax.all_to_all(jnp.stack([user_accum] * lax.axis_size('col')), 'col', 0, 0)]
    dot_general x12, matrix products: 24.8 us -> 20.4 us  [update(): lax.dot_general(user_half, item_half, (((1,), (1,)), ((), ())), preferred...]
  transfers between devices with their start and end apart: 7 -> 7, of which waited for: 5 -> 4; matrix products, arithmetic and copies ran while one was open for 10% -> 7% of each run, Pallas kernels for 0% -> 0%
where the time goes in v1:
time: 258 us; the launch traced here: 257 us
  blocking collectives  75.8 us (29%)
  waiting for transfers between devices  71.9 us (28%)
  matrix products  57.5 us (22%)
  between operations  22.4 us (9%)
  local copies, waits for them, and re-layouts  14.4 us (6%)
  other arithmetic  9.85 us (4%)
  starting transfers between devices  5.48 us (2%)
    psum x1, blocking collectives, on_device(): total_error, total_count = lax.psum((sq_error, observed), ('row', 'col'))  75.8 us
    all_to_all x1, waiting for transfers between devices, on_device(): lax.all_to_all(jnp.stack([user_accum] * lax.axis_size('col')), 'col', 0, 0)  35.6 us
    ppermute x3, waiting for transfers between devices, passed_along(): return lax.ppermute(value, axis, pairs)  35.6 us
    dot_general x12, matrix products, update(): lax.dot_general(user_half, item_half, (((1,), (1,)), ((), ())), preferred...  20.4 us
    dot_general x12, matrix products, update(): jnp.dot(err_half, item_half, preferred_element_type=jnp.float32)  19 us
    dot_general x12, matrix products, update(): lax.dot_general(err_half, user_half, (((0,), (0,)), ((), ())), preferred_...  18.1 us
    all_to_all x1, starting transfers between devices, on_device(): lax.all_to_all(jnp.stack([user_accum] * lax.axis_size('col')), 'col', 0, 0)  5.39 us
  transfers between devices with their start and end apart: 7, of which 4 were waited for; matrix products, arithmetic and copies ran while one was open for 7% of the time, Pallas kernels for 0%

profile of v1, /device:TPU:0, one launch (start us, length us, event | category | flops | bytes accessed | tf_op | source)
XLA Modules:
  0.0 257.3 jit_solution(9082472004228521295)
XLA Ops:
  7.9 2.5 stack.49
  10.4 5.4 %all-to-all-start = ((f32[4,1024,128]{2,1,0:T(8,128)}), f32[4,1024,128]{2,1,0:T(8,128)S(1)}, u32[]{:S(2)}, u32[]{:S(2)}) async-start(f32[4,1024,128]{2,1,0:T(8,128)} %stack.49), calls=%async_computation | async-start | bytes 4194304 | tf_op jit(solution)/shard_map/all_to_all | solution.py:69
  18.6 35.6 %all-to-all-done = f32[4,1024,128]{2,1,0:T(8,128)S(1)} async-done(((f32[4,1024,128]{2,1,0:T(8,128)}), f32[4,1024,128]{2,1,0:T(8,128)S(1)}, u32[]{:S(2)}, u32[]{:S(2)}) %all-to-all-start) | async-done | bytes 2097184 | tf_op jit(solution)/shard_map/all_to_all | solution.py:69
  54.3 1.2 slice-done.8
  55.5 1.6 fusion.37
  58.1 3.6 %multiply_reduce_fusion.3 = (f32[]{:T(128)}, bf16[2048,512]{1,0:T(8,128)(2,1)S(1)}) fusion(f32[256,8,4,128]{3,2,1,0:T(4,128)S(1)} %bitcast.201, bf16[4,2048,512]{2,1,0:T(8,128)(2,1)} %param.7, f32[512,128]{1,0:T(8,128)S(1)} %copy-done.5, f32[2048,128]{1,0:T(8,128)S(1)} %fusion.37), kind=kOutput, calls=%fused_computation.35 | convolution fusion | flops 275054592 | bytes 9699332 | tf_op jit(solution)/shard_map/dot_general | solution.py:23
  65.4 1.7 multiply_subtract_fusion.9
  69.5 2.3 multiply_subtract_fusion.8
  71.8 12.0 %collective-permute-done = f32[2,512,128]{2,1,0:T(8,128)} collective-permute-done((f32[2,512,128]{2,1,0:T(8,128)}, f32[2,512,128]{2,1,0:T(8,128)}, u32[]{:S(2)}, u32[]{:S(2)}) %collective-permute-start) | collective-permute-done | bytes 524320 | tf_op jit(solution)/shard_map/ppermute | solution.py:16
  84.4 3.7 %multiply_reduce_fusion.2 = (f32[]{:T(128)}, bf16[2048,512]{1,0:T(8,128)(2,1)S(1)}) fusion(f32[256,8,4,128]{3,2,1,0:T(4,128)S(1)} %bitcast.204, bf16[4,2048,512]{2,1,0:T(8,128)(2,1)} %param.7, f32[2,512,128]{2,1,0:T(8,128)} %collective-permute-done, f32[2048,128]{1,0:T(8,128)S(1)} %get-tuple-element.33), kind=kOutput, calls=%fused_computation.34 | convolution fusion | flops 274989056 | bytes 9568260 | tf_op jit(solution)/shard_map/dot_general | solution.py:23
  88.1 1.9 multiply_subtract_fusion.17
  90.1 1.7 multiply_subtract_fusion.7
  92.5 1.7 multiply_subtract_fusion.6
  94.2 1.7 multiply_subtract_fusion.16
  100.0 1.9 multiply_subtract_fusion.5
  101.9 11.7 %collective-permute-done.1 = f32[2,512,128]{2,1,0:T(8,128)} collective-permute-done((f32[2,512,128]{2,1,0:T(8,128)}, f32[2,512,128]{2,1,0:T(8,128)}, u32[]{:S(2)}, u32[]{:S(2)}) %collective-permute-start.1) | collective-permute-done | bytes 524320 | tf_op jit(solution)/shard_map/ppermute | solution.py:16
  114.2 3.7 %multiply_reduce_fusion.1 = (f32[]{:T(128)}, bf16[2048,512]{1,0:T(8,128)(2,1)S(1)}) fusion(f32[256,8,4,128]{3,2,1,0:T(4,128)S(1)} %bitcast.207, bf16[4,2048,512]{2,1,0:T(8,128)(2,1)} %param.7, f32[2,512,128]{2,1,0:T(8,128)} %collective-permute-done.1, f32[2048,128]{1,0:T(8,128)S(1)} %get-tuple-element.69), kind=kOutput, calls=%fused_computation.33 | convolution fusion | flops 274989056 | bytes 9568260 | tf_op jit(solution)/shard_map/dot_general | solution.py:23
  117.9 1.9 multiply_subtract_fusion.15
  119.9 1.7 multiply_subtract_fusion.4
  122.5 1.7 multiply_subtract_fusion.3
  124.3 1.7 multiply_subtract_fusion.14
  129.5 2.3 multiply_subtract_fusion.2
  131.8 11.9 %collective-permute-done.2 = f32[2,512,128]{2,1,0:T(8,128)} collective-permute-done((f32[2,512,128]{2,1,0:T(8,128)}, f32[2,512,128]{2,1,0:T(8,128)}, u32[]{:S(2)}, u32[]{:S(2)}) %collective-permute-start.2) | collective-permute-done | bytes 524320 | tf_op jit(solution)/shard_map/ppermute | solution.py:16
  144.3 3.7 %multiply_reduce_fusion = (f32[]{:T(128)}, bf16[2048,512]{1,0:T(8,128)(2,1)S(1)}) fusion(f32[256,8,4,128]{3,2,1,0:T(4,128)S(1)} %bitcast.210, bf16[4,2048,512]{2,1,0:T(8,128)(2,1)} %param.7, f32[2,512,128]{2,1,0:T(8,128)} %collective-permute-done.2, f32[2048,128]{1,0:T(8,128)S(1)} %get-tuple-element.27), kind=kOutput, calls=%fused_computation.32 | convolution fusion | flops 274989056 | bytes 9568260 | tf_op jit(solution)/shard_map/dot_general | solution.py:23
  148.0 1.9 multiply_subtract_fusion.13
  150.0 1.8 multiply_subtract_fusion.1
  153.2 2.4 multiply_subtract_fusion.12
  157.3 1.6 copy-done.3
  159.5 1.5 slice.93
  161.1 3.1 %slice.92 = f32[4096,128]{1,0:T(8,128)} slice(f32[6144,128]{1,0:T(8,128)} %copy-done.3), slice={[0:4096], [0:128]} | slice | bytes 4194304 | tf_op jit(solution)/shard_map/slice | solution.py:107
  166.7 75.8 %all-reduce = (f32[]{:T(128)}, f32[]{:T(128)}, f32[]{:T(128)}, f32[]{:T(128)}, f32[]{:T(128)}, /*index=5*/f32[]{:T(128)}, f32[]{:T(128)}, f32[]{:T(128)}) all-reduce(f32[]{:T(128)} %get-tuple-element.45, f32[]{:T(128)S(6)} %mul.689, f32[]{:T(128)} %get-tuple-element.43, ...), channel_id=1, replica_groups=mesh['row'=32,'col'=4] {'row','col'}, use_global_device_ids=true, to_apply=%region_17.18 | all-reduce | flops 8 | bytes 64 | tf_op jit(solution)/shard_map/psum | solution.py:89
  248.1 2.6 %multiply_subtract_fusion.11 = (f32[512,128]{1,0:T(8,128)}, f32[512,128]{1,0:T(8,128)}) fusion(f32[512,128]{1,0:T(8,128)S(1)} %get-tuple-element.81, f32[512,128]{1,0:T(8,128)} %get-tuple-element.82, f32[512,128]{1,0:T(8,128)} %copy-done.4, f32[2,512,128]{2,1,0:T(8,128)} %collective-permute-done.2, bf16[2048,512]{1,0:T(8,128)(2,1)S(1)} %fusion.15, ...), kind=kOutput, calls=%fused_computation.122 | convolution fusion | flops 269484032 | bytes 4718592 | tf_op jit(solution)/shard_map/dot_general | solution.py:39
  (89 shorter events, 25.3 us)
Async XLA Ops:
  7.2 47.1 %all-gather.2.cloned.1.call-start = ((), (), s32[]{:S(2)}) async-start(), calls=%async_computation.3 | async-start | bytes 2621440 | tf_op jit(solution)/shard_map/all_gather | solution.py:67
  10.4 5.4 %copy-start.8 = (s32[128]{0:T(128)S(1)}, s32[128]{0:T(128)}, u32[]{:S(2)}) copy-start(s32[128]{0:T(128)} %param.9) | copy-start | bytes 1540
  10.4 7.4 %copy-start.7 = (s32[4,16,4]{1,2,0:T(4,128)S(1)}, s32[4,16,4]{1,2,0:T(4,128)}, u32[]{:S(2)}) copy-start(s32[4,16,4]{1,2,0:T(4,128)} %param.8) | copy-start | bytes 3076
  10.4 43.8 %all-to-all-start = ((f32[4,1024,128]{2,1,0:T(8,128)}), f32[4,1024,128]{2,1,0:T(8,128)S(1)}, u32[]{:S(2)}, u32[]{:S(2)}) async-start(f32[4,1024,128]{2,1,0:T(8,128)} %stack.49), calls=%async_computation | async-start | bytes 4194304 | tf_op jit(solution)/shard_map/all_to_all | solution.py:69
  15.8 234.9 %reduce-scatter.5.cloned.1.call-start = ((), (), s32[]{:S(2)}) async-start(), calls=%async_computation.5 | async-start | bytes 2621440 | tf_op jit(solution)/shard_map/reduce_scatter | solution.py:109
  54.3 1.2 slice-start.8
  57.2 1.0 copy-start.5
  58.1 3.6 %copy-start.6 = (f32[512,128]{1,0:T(8,128)S(1)}, f32[512,128]{1,0:T(8,128)}, u32[]{:S(2)}) copy-start(f32[512,128]{1,0:T(8,128)} %param.13) | copy-start | bytes 786436
  58.1 5.2 %slice-start = ((s8[8388608]{0:T(1024)(128)(4,1)}), s8[4194304]{0:T(1024)(128)(4,1)S(1)}, s32[]{:S(2)}) async-start(s8[8388608]{0:T(1024)(128)(4,1)} %bitcast.193), calls=%async_computation.6 | async-start | bytes 8388608
  61.7 2.2 slice-start.1
  63.3 2.1 copy-start
  69.5 14.4 %collective-permute-start = (f32[2,512,128]{2,1,0:T(8,128)}, f32[2,512,128]{2,1,0:T(8,128)}, u32[]{:S(2)}, u32[]{:S(2)}) collective-permute-start(f32[2,512,128]{2,1,0:T(8,128)} %pad_maximum_fusion), channel_id=1, source_target_pairs={{0,1},{1,2},{2,3},{3,4},{4,5},{5,6},{6,7},{7,8},{8,9},{9,10},{10,1... | collective-permute-start | bytes 1572872 | tf_op jit(solution)/shard_map/ppermute | solution.py:16
  84.4 7.3 %slice-start.2 = ((s8[8388608]{0:T(1024)(128)(4,1)}), s8[4194304]{0:T(1024)(128)(4,1)S(1)}, s32[]{:S(2)}) async-start(s8[8388608]{0:T(1024)(128)(4,1)} %bitcast.195), calls=%async_computation.8 | async-start | bytes 8388608
  88.1 3.6 %slice-start.3 = ((s8[8388608]{0:T(1024)(128)(4,1)}), s8[4194304]{0:T(1024)(128)(4,1)S(1)}, s32[]{:S(2)}) async-start(s8[8388608]{0:T(1024)(128)(4,1)} %bitcast.195), calls=%async_computation.9 | async-start | bytes 8388608
  99.3 14.4 %collective-permute-start.1 = (f32[2,512,128]{2,1,0:T(8,128)}, f32[2,512,128]{2,1,0:T(8,128)}, u32[]{:S(2)}, u32[]{:S(2)}) collective-permute-start(f32[2,512,128]{2,1,0:T(8,128)} %pad_maximum_fusion.1), channel_id=1, source_target_pairs={{0,1},{1,2},{2,3},{3,4},{4,5},{5,6},{6,7},{7,8},{8,9},{9,10},{10,1... | collective-permute-start | bytes 1572872 | tf_op jit(solution)/shard_map/ppermute | solution.py:16
  114.2 7.4 %slice-start.4 = ((s8[8388608]{0:T(1024)(128)(4,1)}), s8[4194304]{0:T(1024)(128)(4,1)S(1)}, s32[]{:S(2)}) async-start(s8[8388608]{0:T(1024)(128)(4,1)} %bitcast.197), calls=%async_computation.10 | async-start | bytes 8388608
  117.9 1.9 copy-start.1
  117.9 3.7 %slice-start.5 = ((s8[8388608]{0:T(1024)(128)(4,1)}), s8[4194304]{0:T(1024)(128)(4,1)S(1)}, s32[]{:S(2)}) async-start(s8[8388608]{0:T(1024)(128)(4,1)} %bitcast.197), calls=%async_computation.11 | async-start | bytes 8388608
  121.6 1.0 copy-start.2
  129.3 14.4 %collective-permute-start.2 = (f32[2,512,128]{2,1,0:T(8,128)}, f32[2,512,128]{2,1,0:T(8,128)}, u32[]{:S(2)}, u32[]{:S(2)}) collective-permute-start(f32[2,512,128]{2,1,0:T(8,128)} %pad_maximum_fusion.2), channel_id=1, source_target_pairs={{0,1},{1,2},{2,3},{3,4},{4,5},{5,6},{6,7},{7,8},{8,9},{9,10},{10,1... | collective-permute-start | bytes 1572872 | tf_op jit(solution)/shard_map/ppermute | solution.py:16
  144.3 7.5 %slice-start.6 = ((s8[8388608]{0:T(1024)(128)(4,1)}), s8[4194304]{0:T(1024)(128)(4,1)S(1)}, s32[]{:S(2)}) async-start(s8[8388608]{0:T(1024)(128)(4,1)} %bitcast.199), calls=%async_computation.12 | async-start | bytes 8388608
  148.0 3.7 %slice-start.7 = ((s8[8388608]{0:T(1024)(128)(4,1)}), s8[4194304]{0:T(1024)(128)(4,1)S(1)}, s32[]{:S(2)}) async-start(s8[8388608]{0:T(1024)(128)(4,1)} %bitcast.199), calls=%async_computation.13 | async-start | bytes 8388608
  150.0 3.3 %copy-start.4 = (f32[512,128]{1,0:T(8,128)}, f32[512,128]{1,0:T(8,128)S(1)}, u32[]{:S(2)}) copy-start(f32[512,128]{1,0:T(8,128)S(1)} %get-tuple-element.80) | copy-start | bytes 786436
  157.3 1.6 copy-start.3
  161.0 89.7 %reduce-scatter.3.cloned.1.call-start = ((), (), s32[]{:S(2)}) async-start(), calls=%async_computation.4 | async-start | bytes 2621440 | tf_op jit(solution)/shard_map/reduce_scatter | solution.py:106
Sparse Core Ops, SparseCore 0:
  9.6 40.5 all-gather.1
  161.1 31.7 reduce-scatter.4
  196.1 37.6 reduce-scatter.2
